TPU v7x, 256 devices: a whole 4x4x8 slice. The times are simulated.
256 devices in a mesh: gx: 16 (over z, core), gy: 16 (over x, y).
Axes of the slice: x: 4, y: 4, z: 8, core: 2. Of those that a mesh axis runs over, the one named last changes fastest.
Arguments:
- state: bfloat16 [2, 256, 768, 2048], P(None, None, 'gx', 'gy'), as said below
Outputs:
- modes: bfloat16 [255, 2, 768, 2048], P(None, None, 'gx', 'gy')
- reduced: float32 [255, 255], replicated
Inputs may be any that keep to these rules, and one draw needn't show every extreme that they name: `state`: both fields are positive.
All inputs are finite; a program needn't handle non-finite values.
Results may differ from a plain program's by a relative error of at most 0.0077.
Values may be sent and summed in bfloat16 or wider, within the bound.
No kernel may reach another device: no remote copies, remote signals or barrier semaphores. Data moves between devices by JAX's collectives and lax.ppermute only.
A program may use at most 128 MiB of HBM per device.

v0:
```python
import jax
import jax.numpy as jnp
from jax import lax
from jax.sharding import PartitionSpec as P


def padded_2(cells, sides, width):
    for axis, dim in sides:
        count = lax.axis_size(axis)
        ends = count - 1
        head = lax.slice_in_dim(cells, 0, width, axis=dim)
        tail = lax.slice_in_dim(cells, cells.shape[dim] - width, cells.shape[dim], axis=dim)
        cells = jnp.concatenate(
            [
                lax.ppermute(tail, axis, [(i, (i + 1) % count) for i in range(ends)]),
                cells,
                lax.ppermute(head, axis, [((i + 1) % count, i) for i in range(ends)]),
            ],
            axis=dim,
        )
    return cells


def tri_solve(lower, right):
    return lax.linalg.triangular_solve(lower, right, left_side=True, lower=True)


def gradients(padded):
    grad_x = (
        padded[:, :-4, 2:-2]
        - 8.0 * padded[:, 1:-3, 2:-2]
        + 8.0 * padded[:, 3:-1, 2:-2]
        - padded[:, 4:, 2:-2]
    ) / 12.0
    grad_y = (
        padded[:, 2:-2, :-4]
        - 8.0 * padded[:, 2:-2, 1:-3]
        + 8.0 * padded[:, 2:-2, 3:-1]
        - padded[:, 2:-2, 4:]
    ) / 12.0
    return jnp.stack([grad_x, grad_y], axis=1).astype(jnp.bfloat16)


def shards(state):
    snaps = state.shape[1]
    rows_x = state.shape[2]
    rows_y = state.shape[3]
    total_rows = 2 * rows_x * rows_y * lax.axis_size("gx") * lax.axis_size("gy")
    temp = 0.4 * state[1].astype(jnp.float32) / state[0].astype(jnp.float32)
    padded = padded_2(temp, (("gx", 1), ("gy", 2)), 2)
    features = gradients(padded)
    snap = features.reshape(snaps, 2 * rows_x * rows_y)
    local_gram = (
        lax.dot_general(snap, snap, (((1,), (1,)), ((), ())), preferred_element_type=jnp.float32)
        / total_rows
    )
    gram = lax.psum(local_gram, ("gx", "gy"))
    lower = jnp.linalg.cholesky(gram[: snaps - 1, : snaps - 1])
    cross = gram[: snaps - 1, 1:]
    half = tri_solve(lower, cross)
    reduced = tri_solve(lower, half.T).T
    inverse = tri_solve(lower, jnp.eye(snaps - 1, dtype=jnp.float32)).astype(jnp.bfloat16)
    modes = jnp.dot(inverse, snap[1:], preferred_element_type=jnp.float32).astype(jnp.bfloat16)
    return (modes.reshape(snaps - 1, 2, rows_x, rows_y), reduced)


def solution(mesh):
    placed = (P(None, None, "gx", "gy"),)
    return jax.shard_map(
        shards,
        mesh=mesh,
        in_specs=placed,
        out_specs=(P(None, None, "gx", "gy"), P()),
        check_vma=False,
    )
```

profile of v0, /device:TPU:2, one launch (start us, length us, event | category | flops | bytes accessed | tf_op | source)
XLA Modules:
  0.0 435.9 jit_solution(15575594914575890213)
XLA Ops:
  7.2 3.9 fusion.44
  11.1 1.3 divide_bitcast_fusion
  12.5 1.8 collective-permute-start
  14.3 1.3 collective-permute-start.1
  16.3 3.1 collective-permute-done.1
  20.1 3.6 pad_maximum_fusion.1
  23.7 11.6 %fusion.42 = (f32[256,52,2]{2,0,1:T(8,128)}, f32[256,52,2]{2,0,1:T(8,128)}) fusion(f32[256,52,128]{2,0,1:T(8,128)} %pad_maximum_fusion.1), kind=kLoop, calls=%fused_computation.88 | loop fusion | bytes 425984 | tf_op jit(solution)/shard_map/slice | solution.py:12
  35.4 4.7 %copy.16 = f32[256,52,2]{0,2,1:T(2,128)S(1)} copy(f32[256,52,2]{2,0,1:T(8,128)} %get-tuple-element.41) | data formatting | bytes 212992 | tf_op jit(solution)/shard_map/slice | solution.py:12
  40.1 3.5 collective-permute-start.2
  43.6 5.3 %copy.18 = f32[256,52,2]{0,2,1:T(2,128)} copy(f32[256,52,2]{2,0,1:T(8,128)} %get-tuple-element.42) | data formatting | bytes 212992 | tf_op jit(solution)/shard_map/slice | solution.py:11
  48.9 4.6 %collective-permute-start.3 = (f32[256,52,2]{0,2,1:T(2,128)}, f32[256,52,2]{0,2,1:T(2,128)}, u32[]{:S(2)}, u32[]{:S(2)}) collective-permute-start(f32[256,52,2]{0,2,1:T(2,128)} %copy.18), channel_id=1, source_target_pairs={{1,0},{2,1},{3,2},{4,3},{5,4},{6,5},{7,6},{8,7},{9,8},{10,9},{11,1... | collective-permute-start | bytes 319496 | tf_op jit(solution)/shard_map/ppermute | solution.py:17
  53.5 11.1 %fusion.17 = bf16[256,1,48,128]{3,0,2,1:T(8,128)(2,1)S(1)} fusion(f32[256,2,128]{2,0,1:T(8,128)} %copy-done.2, f32[256,48,128]{2,0,1:T(8,128)} %copy-done, f32[256,2,128]{2,0,1:T(8,128)S(1)} %collective-permute-done), kind=kLoop, calls=%fused_computation.36 | loop fusion | flops 17301504 | bytes 9961472 | tf_op jit(solution)/shard_map/stack | solution.py:41
  64.6 5.0 %copy.17 = f32[256,52,2]{2,0,1:T(8,128)} copy(f32[256,52,2]{0,2,1:T(2,128)} %collective-permute-done.2) | data formatting | bytes 212992 | tf_op jit(solution)/shard_map/ppermute | solution.py:15
  69.6 5.1 %copy.19 = f32[256,52,2]{2,0,1:T(8,128)} copy(f32[256,52,2]{0,2,1:T(2,128)} %collective-permute-done.3) | data formatting | bytes 212992 | tf_op jit(solution)/shard_map/ppermute | solution.py:17
  74.7 21.0 %fusion.18 = bf16[256,1,48,128]{3,0,2,1:T(8,128)(2,1)S(1)} fusion(f32[256,52,2]{2,0,1:T(8,128)} %copy.19, f32[256,2,128]{2,0,1:T(8,128)} %copy-done.2, f32[256,48,128]{2,0,1:T(8,128)} %copy-done, f32[256,2,128]{2,0,1:T(8,128)S(1)} %collective-permute-done, f32[256,52,2]{2,0,1:T(8,128)} %copy.17), kind=kLoop, calls=%fused_computation.37 | loop fusion | flops 29884416 | bytes 10174464 | tf_op jit(solution)/shard_map/stack | solution.py:41
  95.8 1.7 copy-done.1
  97.4 2.5 fusion.20
  100.0 5.9 %fusion.8 = bf16[255,2,48,128]{3,0,2,1:T(8,128)(2,1)} fusion(bf16[256,1,48,128]{3,0,2,1:T(8,128)(2,1)S(1)} %fusion.17, bf16[256,1,48,128]{3,0,2,1:T(8,128)(2,1)} %copy-done.1), kind=kLoop, calls=%fused_computation.17 | loop fusion | flops 3133440 | bytes 12558336 | tf_op jit(solution)/shard_map/stack | solution.py:41
  105.8 8.7 %copy.22 = bf16[255,2,48,128]{0,3,2,1:T(8,128)(2,1)} copy(bf16[255,2,48,128]{3,0,2,1:T(8,128)(2,1)} %fusion.8) | data formatting | bytes 12533760 | tf_op jit(solution)/shard_map/slice | solution.py:63
  114.5 240.5 %all-reduce.4.cloned.1.call-done = f32[256,256]{0,1:T(8,128)} async-done(((f32[256,256]{0,1:T(8,128)}), f32[256,256]{0,1:T(8,128)}) %all-reduce.4.cloned.1.call-update) | async-done | bytes 262160 | tf_op jit(solution)/shard_map/psum | solution.py:57
  355.0 1.1 copy.21
  356.1 1.0 fusion.21
  357.1 11.7 %cholesky.51 = f32[128,128]{1,0:T(8,128)S(1)} custom-call(f32[128,128]{1,0:T(8,128)S(1)} %cholesky.124), custom_call_target="Cholesky" | custom-call | tf_op jit(solution)/shard_map/jit(cholesky)/cholesky | solution.py:58
  368.9 9.8 %custom-call.14 = f32[1,128,128]{1,2,0:T(8,128)S(1)} custom-call(f32[1,128,128]{2,1,0:T(8,128)S(1)} %get-tuple-element.50), custom_call_target="InvertDiagBlocksLowerTriangular" | custom-call | tf_op jit(solution)/shard_map/jit(cholesky)/cholesky | solution.py:58
  379.2 11.6 %cholesky.110 = f32[127,127]{1,0:T(8,128)S(1)} custom-call(f32[127,127]{1,0:T(8,128)S(1)} %convolution_subtract_fusion.2), custom_call_target="Cholesky" | custom-call | tf_op jit(solution)/shard_map/jit(cholesky)/cholesky | solution.py:58
  393.6 19.9 %custom-call.17 = f32[2,128,128]{1,2,0:T(8,128)S(1)} custom-call(f32[2,128,128]{2,1,0:T(8,128)S(1)} %pad_maximum_fusion.15), custom_call_target="InvertDiagBlocksLowerTriangular" | custom-call | tf_op jit(solution)/shard_map/triangular_solve/custom-call.0 | solution.py:25
  413.5 1.2 fusion.26
  415.1 1.2 fusion.25
  417.4 0.8 copy.25
  419.2 4.6 %convolution_convert_fusion = bf16[255,12288]{1,0:T(8,128)(2,1)S(1)} fusion(bf16[255,12288]{0,1:T(8,128)(2,1)} %bitcast.61, bf16[127,255]{1,0:T(8,128)(2,1)S(1)} %fusion.35, f32[128,255]{1,0:T(8,128)S(1)} %fusion.28), kind=kOutput, calls=%fused_computation | convolution fusion | flops 1601447936 | bytes 12729090 | tf_op jit(solution)/shard_map/dot_general | solution.py:63
  423.8 1.5 copy.32
  425.3 3.8 slice.212
  (37 shorter events, 5.8 us)
Async XLA Ops:
  7.2 347.8 %all-reduce.4.cloned.1.call-start = ((), (), s32[]{:S(2)}) async-start(), calls=%async_computation | async-start | bytes 524288 | tf_op jit(solution)/shard_map/psum | solution.py:57
  12.5 6.9 %copy-start = (f32[256,48,128]{2,0,1:T(8,128)}, f32[256,48,128]{2,0,1:T(8,128)S(1)}, u32[]{:S(2)}) copy-start(f32[256,48,128]{2,0,1:T(8,128)S(1)} %divide_bitcast_fusion) | copy-start | bytes 18874372
  12.5 3.8 collective-permute-start
  14.3 5.1 %collective-permute-start.1 = (f32[256,2,128]{2,0,1:T(8,128)S(1)}, f32[256,2,128]{2,0,1:T(8,128)S(1)}, u32[]{:S(2)}, u32[]{:S(2)}) collective-permute-start(f32[256,2,128]{2,0,1:T(8,128)S(1)} %get-tuple-element.44), channel_id=1, source_target_pairs={{16,0},{32,16},{48,32},{64,48},{80,64},{96,80},{112,96},{128,112},... | collective-permute-start | bytes 786440 | tf_op jit(solution)/shard_map/ppermute | solution.py:17
  19.4 0.7 copy-start.2
  40.1 24.5 %collective-permute-start.2 = (f32[256,52,2]{0,2,1:T(2,128)S(1)}, f32[256,52,2]{0,2,1:T(2,128)}, u32[]{:S(2)}, u32[]{:S(2)}) collective-permute-start(f32[256,52,2]{0,2,1:T(2,128)S(1)} %copy.16), channel_id=1, source_target_pairs={{0,1},{1,2},{2,3},{3,4},{4,5},{5,6},{6,7},{7,8},{8,9},{9,10},{10,1... | collective-permute-start | bytes 319496 | tf_op jit(solution)/shard_map/ppermute | solution.py:15
  48.9 20.7 %collective-permute-start.3 = (f32[256,52,2]{0,2,1:T(2,128)}, f32[256,52,2]{0,2,1:T(2,128)}, u32[]{:S(2)}, u32[]{:S(2)}) collective-permute-start(f32[256,52,2]{0,2,1:T(2,128)} %copy.18), channel_id=1, source_target_pairs={{1,0},{2,1},{3,2},{4,3},{5,4},{6,5},{7,6},{8,7},{9,8},{10,9},{11,1... | collective-permute-start | bytes 319496 | tf_op jit(solution)/shard_map/ppermute | solution.py:17
  95.8 1.7 copy-start.1
  105.8 287.6 %copy-start.4 = (f32[128,1]{1,0:T(8,128)S(1)}, f32[128,1]{1,0:T(8,128)}, u32[]{:S(2)}) copy-start(f32[128,1]{1,0:T(8,128)} %constant.87.clone.3) | copy-start | bytes 1540
  114.5 303.8 %copy-start.3 = (f32[255,255]{1,0:T(8,128)S(1)}, f32[255,255]{1,0:T(8,128)}, u32[]{:S(2)}) copy-start(f32[255,255]{1,0:T(8,128)} %fusion.22) | copy-start | bytes 780304
Sparse Core Ops, SparseCore 0:
  100.1 254.8 all-reduce.3
where the time goes:
time: 437 us; the launch traced here: 436 us
  waiting for transfers between devices  244 us (56%)
  other arithmetic  99.2 us (23%)
  local copies, waits for them, and re-layouts  53.9 us (12%)
  between operations  15.6 us (4%)
  matrix products  12.3 us (3%)
  starting transfers between devices  11.2 us (3%)
    psum x1, waiting for transfers between devices, shards(): gram = lax.psum(local_gram, ('gx', 'gy'))  240 us
    another operation x3, other arithmetic, gradients(): return jnp.stack([grad_x, grad_y], axis=1).astype(jnp.bfloat16)  38 us
    another operation x7, other arithmetic, shards(): lower = jnp.linalg.cholesky(gram[:snaps - 1, :snaps - 1])  34.5 us
    another operation x4, other arithmetic, tri_solve(): return lax.linalg.triangular_solve(lower, right, left_side=True, lower=True)  20.1 us
    slice x3, local copies, waits for them, and re-layouts, padded_2(): lax.slice_in_dim(cells, cells.shape[dim] - width, cells.shape[dim], axis=...  16.4 us
  transfers between devices with their start and end apart: 5, of which 2 were waited for; matrix products, arithmetic and copies ran while one was open for 8% of the time, Pallas kernels for 0%

commit v1 on v0

--- a/solution.py
+++ b/solution.py
@@ -54,7 +54,8 @@
         lax.dot_general(snap, snap, (((1,), (1,)), ((), ())), preferred_element_type=jnp.float32)
         / total_rows
     )
-    gram = lax.psum(local_gram, ("gx", "gy"))
+    shards_2 = lax.all_gather(local_gram, ("gx", "gy"))
+    gram = jnp.sum(shards_2, axis=0)
     lower = jnp.linalg.cholesky(gram[: snaps - 1, : snaps - 1])
     cross = gram[: snaps - 1, 1:]
     half = tri_solve(lower, cross)

time: 437 us -> 418 us (0.957)
  waiting for transfers between devices: 244 us -> 207 us
  other arithmetic: 99.2 us -> 119 us
    psum x1 -> x0, waiting for transfers between devices: 240 us -> none  [shards(): gram = lax.psum(local_gram, ('gx', 'gy'))]
    all_gather x0 -> x1, waiting for transfers between devices: none -> 203 us  [shards(): shards_2 = lax.all_gather(local_gram, ('gx', 'gy'))]
    reduce_sum x0 -> x1, other arithmetic: none -> 21.3 us  [shards(): gram = jnp.sum(shards_2, axis=0)]
  transfers between devices with their start and end apart: 5 -> 5, of which waited for: 2 -> 2; matrix products, arithmetic and copies ran while one was open for 8% -> 9% of each run, Pallas kernels for 0% -> 0%
where the time goes in v1:
time: 418 us; the launch traced here: 416 us
  waiting for transfers between devices  207 us (50%)
  other arithmetic  119 us (28%)
  local copies, waits for them, and re-layouts  52.9 us (13%)
  between operations  15.6 us (4%)
  starting transfers between devices  11.2 us (3%)
  matrix products  10.4 us (2%)
    all_gather x1, waiting for transfers between devices, shards(): shards_2 = lax.all_gather(local_gram, ('gx', 'gy'))  203 us
    another operation x3, other arithmetic, gradients(): return jnp.stack([grad_x, grad_y], axis=1).astype(jnp.bfloat16)  38.2 us
    another operation x7, other arithmetic, shards(): lower = jnp.linalg.cholesky(gram[:snaps - 1, :snaps - 1])  34.5 us
    reduce_sum x1, other arithmetic, shards(): gram = jnp.sum(shards_2, axis=0)  21.3 us
    another operation x4, other arithmetic, tri_solve(): return lax.linalg.triangular_solve(lower, right, left_side=True, lower=True)  20.1 us
    slice x3, local copies, waits for them, and re-layouts, padded_2(): lax.slice_in_dim(cells, cells.shape[dim] - width, cells.shape[dim], axis=...  16.4 us
    slice x1, local copies, waits for them, and re-layouts, shards(): snap[1:]  8.65 us
    unnamed x12, local copies, waits for them, and re-layouts  8.57 us
  transfers between devices with their start and end apart: 5, of which 2 were waited for; matrix products, arithmetic and copies ran while one was open for 9% of the time, Pallas kernels for 0%

profile of v1, /device:TPU:2, one launch (start us, length us, event | category | flops | bytes accessed | tf_op | source)
XLA Modules:
  0.0 415.8 jit_solution(17109932778498276445)
XLA Ops:
  7.2 3.9 fusion.43
  11.1 1.3 divide_bitcast_fusion
  12.5 1.8 collective-permute-start
  14.3 1.3 collective-permute-start.1
  15.6 3.8 collective-permute-done.1
  19.4 0.7 copy-done.2
  20.1 3.6 pad_maximum_fusion.1
  23.7 11.6 %fusion.41 = (f32[256,52,2]{2,0,1:T(8,128)}, f32[256,52,2]{2,0,1:T(8,128)}) fusion(f32[256,52,128]{2,0,1:T(8,128)} %pad_maximum_fusion.1), kind=kLoop, calls=%fused_computation.87 | loop fusion | bytes 425984 | tf_op jit(solution)/shard_map/slice | solution.py:12
  35.4 4.7 %copy.14 = f32[256,52,2]{0,2,1:T(2,128)S(1)} copy(f32[256,52,2]{2,0,1:T(8,128)} %get-tuple-element.41) | data formatting | bytes 212992 | tf_op jit(solution)/shard_map/slice | solution.py:12
  40.1 3.5 collective-permute-start.2
  43.6 5.3 %copy.16 = f32[256,52,2]{0,2,1:T(2,128)} copy(f32[256,52,2]{2,0,1:T(8,128)} %get-tuple-element.42) | data formatting | bytes 212992 | tf_op jit(solution)/shard_map/slice | solution.py:11
  48.9 4.6 %collective-permute-start.3 = (f32[256,52,2]{0,2,1:T(2,128)}, f32[256,52,2]{0,2,1:T(2,128)}, u32[]{:S(2)}, u32[]{:S(2)}) collective-permute-start(f32[256,52,2]{0,2,1:T(2,128)} %copy.16), channel_id=1, source_target_pairs={{1,0},{2,1},{3,2},{4,3},{5,4},{6,5},{7,6},{8,7},{9,8},{10,9},{11,1... | collective-permute-start | bytes 319496 | tf_op jit(solution)/shard_map/ppermute | solution.py:17
  53.5 11.1 %fusion.17 = bf16[256,1,48,128]{3,0,2,1:T(8,128)(2,1)S(1)} fusion(f32[256,2,128]{2,0,1:T(8,128)} %copy-done.2, f32[256,48,128]{2,0,1:T(8,128)} %copy-done, f32[256,2,128]{2,0,1:T(8,128)S(1)} %collective-permute-done), kind=kLoop, calls=%fused_computation.36 | loop fusion | flops 17301504 | bytes 9961472 | tf_op jit(solution)/shard_map/stack | solution.py:41
  64.6 5.0 %copy.15 = f32[256,52,2]{2,0,1:T(8,128)} copy(f32[256,52,2]{0,2,1:T(2,128)} %collective-permute-done.2) | data formatting | bytes 212992 | tf_op jit(solution)/shard_map/ppermute | solution.py:15
  69.6 5.1 %copy.17 = f32[256,52,2]{2,0,1:T(8,128)} copy(f32[256,52,2]{0,2,1:T(2,128)} %collective-permute-done.3) | data formatting | bytes 212992 | tf_op jit(solution)/shard_map/ppermute | solution.py:17
  74.7 21.3 %fusion.18 = bf16[256,1,48,128]{3,0,2,1:T(8,128)(2,1)S(1)} fusion(f32[256,52,2]{2,0,1:T(8,128)} %copy.17, f32[256,2,128]{2,0,1:T(8,128)} %copy-done.2, f32[256,48,128]{2,0,1:T(8,128)} %copy-done, f32[256,2,128]{2,0,1:T(8,128)S(1)} %collective-permute-done, f32[256,52,2]{2,0,1:T(8,128)} %copy.15), kind=kLoop, calls=%fused_computation.37 | loop fusion | flops 29884416 | bytes 10174464 | tf_op jit(solution)/shard_map/stack | solution.py:41
  96.0 1.7 copy-done.1
  97.6 2.5 fusion.20
  100.2 5.9 %fusion.8 = bf16[255,2,48,128]{3,0,2,1:T(8,128)(2,1)} fusion(bf16[256,1,48,128]{3,0,2,1:T(8,128)(2,1)S(1)} %fusion.17, bf16[256,1,48,128]{3,0,2,1:T(8,128)(2,1)} %copy-done.1), kind=kLoop, calls=%fused_computation.17 | loop fusion | flops 3133440 | bytes 12558336 | tf_op jit(solution)/shard_map/stack | solution.py:41
  106.1 8.6 %copy.20 = bf16[255,2,48,128]{0,3,2,1:T(8,128)(2,1)} copy(bf16[255,2,48,128]{3,0,2,1:T(8,128)(2,1)} %fusion.8) | data formatting | bytes 12533760 | tf_op jit(solution)/shard_map/slice | solution.py:64
  114.7 202.7 %all-gather.3.cloned.1.call-done = f32[65536,256]{1,0:T(8,128)} async-done(((f32[256,256]{1,0:T(8,128)}), f32[65536,256]{1,0:T(8,128)}) %all-gather.3.cloned.1.call-update) | async-done | bytes 67108880 | tf_op jit(solution)/shard_map/all_gather | solution.py:57
  317.4 21.3 %reduce_sum.9 = f32[256,256]{1,0:T(8,128)S(1)} reduce(f32[256,256,256]{2,1,0:T(8,128)} %bitcast.5, f32[]{:T(128)} %constant.93.clone.1), dimensions={0}, to_apply=%region_0.0 | reduce | flops 16711680 | bytes 67371008 | tf_op jit(solution)/shard_map/reduce_sum | solution.py:58
  338.9 11.7 %cholesky.51 = f32[128,128]{1,0:T(8,128)S(1)} custom-call(f32[128,128]{1,0:T(8,128)S(1)} %cholesky.124), custom_call_target="Cholesky" | custom-call | tf_op jit(solution)/shard_map/jit(cholesky)/cholesky | solution.py:59
  350.7 9.8 %custom-call.14 = f32[1,128,128]{1,2,0:T(8,128)S(1)} custom-call(f32[1,128,128]{2,1,0:T(8,128)S(1)} %get-tuple-element.50), custom_call_target="InvertDiagBlocksLowerTriangular" | custom-call | tf_op jit(solution)/shard_map/jit(cholesky)/cholesky | solution.py:59
  361.0 11.6 %cholesky.110 = f32[127,127]{1,0:T(8,128)S(1)} custom-call(f32[127,127]{1,0:T(8,128)S(1)} %convolution_subtract_fusion.3), custom_call_target="Cholesky" | custom-call | tf_op jit(solution)/shard_map/jit(cholesky)/cholesky | solution.py:59
  372.6 0.6 compare_reduce_fusion
  373.3 0.6 compare_reduce_fusion.1
  375.4 19.9 %custom-call.17 = f32[2,128,128]{1,2,0:T(8,128)S(1)} custom-call(f32[2,128,128]{2,1,0:T(8,128)S(1)} %pad_maximum_fusion.15), custom_call_target="InvertDiagBlocksLowerTriangular" | custom-call | tf_op jit(solution)/shard_map/triangular_solve/custom-call.0 | solution.py:25
  397.4 0.8 copy.22
  399.1 4.6 %convolution_convert_fusion = bf16[255,12288]{1,0:T(8,128)(2,1)S(1)} fusion(bf16[255,12288]{0,1:T(8,128)(2,1)} %bitcast.65, bf16[127,255]{1,0:T(8,128)(2,1)S(1)} %fusion.35, f32[128,255]{1,0:T(8,128)S(1)} %fusion.27), kind=kOutput, calls=%fused_computation | convolution fusion | flops 1601447936 | bytes 12729090 | tf_op jit(solution)/shard_map/dot_general | solution.py:64
  403.7 1.5 copy.28
  405.2 3.8 slice.212
  (36 shorter events, 3.9 us)
Async XLA Ops:
  7.2 310.3 %all-gather.3.cloned.1.call-start = ((), (), s32[]{:S(2)}) async-start(), calls=%async_computation | async-start | bytes 67371008 | tf_op jit(solution)/shard_map/all_gather | solution.py:57
  12.5 6.9 %copy-start = (f32[256,48,128]{2,0,1:T(8,128)}, f32[256,48,128]{2,0,1:T(8,128)S(1)}, u32[]{:S(2)}) copy-start(f32[256,48,128]{2,0,1:T(8,128)S(1)} %divide_bitcast_fusion) | copy-start | bytes 18874372
  12.5 3.1 collective-permute-start
  14.3 5.1 %collective-permute-start.1 = (f32[256,2,128]{2,0,1:T(8,128)S(1)}, f32[256,2,128]{2,0,1:T(8,128)S(1)}, u32[]{:S(2)}, u32[]{:S(2)}) collective-permute-start(f32[256,2,128]{2,0,1:T(8,128)S(1)} %get-tuple-element.44), channel_id=1, source_target_pairs={{16,0},{32,16},{48,32},{64,48},{80,64},{96,80},{112,96},{128,112},... | collective-permute-start | bytes 786440 | tf_op jit(solution)/shard_map/ppermute | solution.py:17
  19.4 0.7 copy-start.2
  40.1 24.5 %collective-permute-start.2 = (f32[256,52,2]{0,2,1:T(2,128)S(1)}, f32[256,52,2]{0,2,1:T(2,128)}, u32[]{:S(2)}, u32[]{:S(2)}) collective-permute-start(f32[256,52,2]{0,2,1:T(2,128)S(1)} %copy.14), channel_id=1, source_target_pairs={{0,1},{1,2},{2,3},{3,4},{4,5},{5,6},{6,7},{7,8},{8,9},{9,10},{10,1... | collective-permute-start | bytes 319496 | tf_op jit(solution)/shard_map/ppermute | solution.py:15
  48.9 20.7 %collective-permute-start.3 = (f32[256,52,2]{0,2,1:T(2,128)}, f32[256,52,2]{0,2,1:T(2,128)}, u32[]{:S(2)}, u32[]{:S(2)}) collective-permute-start(f32[256,52,2]{0,2,1:T(2,128)} %copy.16), channel_id=1, source_target_pairs={{1,0},{2,1},{3,2},{4,3},{5,4},{6,5},{7,6},{8,7},{9,8},{10,9},{11,1... | collective-permute-start | bytes 319496 | tf_op jit(solution)/shard_map/ppermute | solution.py:17
  96.0 1.7 copy-start.1
  317.4 57.8 %copy-start.3 = (f32[128,1]{1,0:T(8,128)S(1)}, f32[128,1]{1,0:T(8,128)}, u32[]{:S(2)}) copy-start(f32[128,1]{1,0:T(8,128)} %constant.88.clone.3) | copy-start | bytes 1540
Sparse Core Ops, SparseCore 0:
  100.3 217.0 all-gather.2
